TPU v7x, 256 devices: a whole 4x4x8 slice. The times are simulated.
256 devices in a mesh: row: 32 (over y, x, core), col: 8 (over z).
Axes of the slice: x: 4, y: 4, z: 8, core: 2. Of those that a mesh axis runs over, the one named last changes fastest.
Arguments:
- start_block: float32 [8192, 256], P(('col', 'row')), may hold values from -6 to 6
- tile_values: float32 [32, 8, 2, 256, 256], P('row', 'col'), may hold values from -0.0625 to 0.0625
- tile_rows: int32 [32, 8, 2], P('row', 'col'), may hold values from 0 to 0, as said below
- tile_cols: int32 [32, 8, 2], P('row', 'col'), may hold values from 0 to 3
- tile_count: int32 [32, 8], P('row', 'col'), may hold values from 1 to 2, as said below
Outputs:
- image_block: float32 [8192, 256], P('row')
- new_basis: float32 [8192, 256], P(('col', 'row'))
- factor: float32 [256, 256], replicated
Inputs may be any that keep to these rules, and one draw needn't show every extreme that they name: On each device the slots name distinct positions (tile_rows, tile_cols) of its 1 x 4 grid of blocks, slots at or beyond tile_count included. `tile_count`: some devices hold exactly 2 live tiles.
All inputs are finite; a program needn't handle non-finite values.
Results may differ from a plain program's by a relative error of at most 0.0001.
Values sent between devices are 32-bit elements; how exact they have to be, the bound alone decides.
No kernel may reach another device: no remote copies, remote signals or barrier semaphores. Data moves between devices by JAX's collectives and lax.ppermute only.
A program may use at most 64 MiB of HBM per device.

v0:
```python
import jax
import jax.numpy as jnp
from jax import lax
from jax.sharding import PartitionSpec as P

BR = 1


def cholesky_lower(gram):
    size = gram.shape[0]
    index = jnp.arange(size, dtype=jnp.int32)

    def column_step(j, lower):
        known = lower * (index[None, :] < j).astype(gram.dtype)
        row_j = lax.dynamic_slice_in_dim(known, j, 1, 0)[0]
        column = lax.dynamic_slice_in_dim(gram, j, 1, 1)[:, 0] - jnp.dot(
            known, row_j, precision=lax.Precision.HIGHEST
        )
        pivot = jnp.sqrt(lax.dynamic_slice_in_dim(column, j, 1, 0)[0])
        column = jnp.where(index >= j, column / pivot, jnp.zeros_like(column))
        return lax.dynamic_update_slice_in_dim(lower, column[:, None], j, 1)

    return lax.fori_loop(0, size, column_step, jnp.zeros_like(gram))


def lower_inverse(lower):
    size = lower.shape[0]
    index = jnp.arange(size, dtype=jnp.int32)

    def row_step(i, inverse):
        row_l = lax.dynamic_slice_in_dim(lower, i, 1, 0)[0]
        known = row_l * (index < i).astype(lower.dtype)
        unit = (index == i).astype(lower.dtype)
        pivot = lax.dynamic_slice_in_dim(row_l, i, 1, 0)[0]
        new_row = (unit - jnp.dot(known, inverse, precision=lax.Precision.HIGHEST)) / pivot
        return lax.dynamic_update_slice_in_dim(inverse, new_row[None, :], i, 0)

    return lax.fori_loop(0, size, row_step, jnp.zeros_like(lower))


def body(start_block, tile_values, tile_rows, tile_cols, tile_count):
    tile_size = tile_values.shape[-1]
    basis_width = start_block.shape[1]
    slot_total = tile_values.shape[2]
    slab = lax.all_gather(start_block, "row", axis=0, tiled=True)
    start_blocks = slab.reshape(-1, tile_size, basis_width)
    block_cols = start_blocks.shape[0]
    values = tile_values.reshape(slot_total, tile_size, tile_size)
    row_ids = tile_rows.reshape(slot_total)
    col_ids = tile_cols.reshape(slot_total)
    live_count = tile_count.reshape(())
    block_rows = BR
    live_mask = (jnp.arange(slot_total, dtype=jnp.int32) < live_count).astype(jnp.float32)
    row_onehot = (row_ids[:, None] == jnp.arange(block_rows, dtype=jnp.int32)[None, :]).astype(
        jnp.float32
    ) * live_mask[:, None]
    products = jnp.einsum(
        "tij,tjk->tik",
        values,
        start_blocks[col_ids],
        precision=lax.Precision.HIGHEST,
        preferred_element_type=jnp.float32,
    )
    partial_image = jnp.einsum(
        "tb,tik->bik",
        row_onehot,
        products,
        precision=lax.Precision.HIGHEST,
        preferred_element_type=jnp.float32,
    )
    partial_rows = partial_image.reshape(-1, basis_width)
    image_block = lax.psum(partial_rows, "col")
    image_blocks = image_block.reshape(block_rows, tile_size, basis_width)
    col_onehot = (col_ids[:, None] == jnp.arange(block_cols, dtype=jnp.int32)[None, :]).astype(
        jnp.float32
    ) * live_mask[:, None]
    back_products = jnp.einsum(
        "tji,tjk->tik",
        values,
        image_blocks[row_ids],
        precision=lax.Precision.HIGHEST,
        preferred_element_type=jnp.float32,
    )
    partial_projected = jnp.einsum(
        "tc,tik->cik",
        col_onehot,
        back_products,
        precision=lax.Precision.HIGHEST,
        preferred_element_type=jnp.float32,
    )
    partial_flat = partial_projected.reshape(-1, basis_width)
    projected = lax.psum_scatter(partial_flat, "row", scatter_dimension=0, tiled=True)
    share_rows = projected.shape[0]
    matrix_order = share_rows * lax.axis_size("row") * lax.axis_size("col")
    local_gram = jnp.dot(
        projected.T, projected, precision=lax.Precision.HIGHEST, preferred_element_type=jnp.float32
    )
    gram_matrix = lax.psum(local_gram, ("row", "col")) / matrix_order
    lower = cholesky_lower(gram_matrix)
    inverse = lower_inverse(lower)
    factor = lower.T
    new_basis = jnp.dot(
        projected, inverse.T, precision=lax.Precision.HIGHEST, preferred_element_type=jnp.float32
    )
    return (image_block, new_basis, factor)


def solution(mesh):
    placed = (
        P(("col", "row"), None),
        P("row", "col", None, None, None),
        P("row", "col", None),
        P("row", "col", None),
        P("row", "col"),
    )
    return jax.shard_map(
        body,
        mesh=mesh,
        in_specs=placed,
        out_specs=(P("row", None), P(("col", "row"), None), P()),
        check_vma=False,
    )
```

profile of v0, /device:TPU:2, one launch (start us, length us, event | category | flops | bytes accessed | tf_op | source)
XLA Modules:
  0.0 1525.9 jit_solution(4812023314239359038)
XLA Ops:
  7.2 0.7 all-gather.2.cloned.1.call-update
  8.7 52.4 %all-gather.2.cloned.1.call-done = f32[1024,256]{1,0:T(8,128)} async-done(((f32[32,256]{1,0:T(8,128)}), f32[1024,256]{1,0:T(8,128)}) %all-gather.2.cloned.1.call-update) | async-done | bytes 1048592 | tf_op jit(solution)/shard_map/all_gather | solution.py:45
  61.0 1.8 gather_fusion
  62.8 1.0 convolution_bitcast_fusion.1
  64.8 1.8 fusion.22
  66.6 0.7 copy.30
  67.4 72.3 %all-reduce.3.cloned.1.call-done = f32[256,256]{1,0:T(8,128)} async-done(((f32[256,256]{1,0:T(8,128)}), f32[256,256]{1,0:T(8,128)}) %all-reduce.3.cloned.1.call-update) | async-done | bytes 262160 | tf_op jit(solution)/shard_map/psum | solution.py:72
  139.7 1.1 copy.21
  141.6 2.3 fusion.14
  143.9 1.2 copy.23
  145.2 83.4 %reduce-scatter.2.cloned.1.call-done = f32[32,256]{1,0:T(8,128)} async-done(((f32[1024,256]{1,0:T(8,128)}), f32[32,256]{1,0:T(8,128)}) %reduce-scatter.2.cloned.1.call-update) | async-done | bytes 32784 | tf_op jit(solution)/shard_map/reduce_scatter | solution.py:92
  228.5 2.0 fusion.30
  230.5 254.0 %all-reduce.5.cloned.1.call-done = f32[256,256]{1,0:T(8,128)} async-done(((f32[256,256]{1,0:T(8,128)}), f32[256,256]{1,0:T(8,128)}) %all-reduce.5.cloned.1.call-update) | async-done | bytes 262160 | tf_op jit(solution)/shard_map/psum | solution.py:98
  484.5 1.0 broadcast_multiply_fusion.1
  485.6 631.3 %while.33 = (s32[]{:T(128)}, f32[256,256]{1,0:T(8,128)S(1)}, f32[256,256]{0,1:T(8,128)S(1)}, s32[]{:T(128)}, s32[]{:T(128)}) while((s32[]{:T(128)}, f32[256,256]{1,0:T(8,128)S(1)}, f32[256,256]{0,1:T(8,128)S(1)}, s32[]{:T(128)}, s32[]{:T(128)}) %tuple.82), condition=%wide.region_4.5_spmd.clone.clone, body=%wide.region_3.4_spmd.clone.clone.sunk | while | flops 853506 | bytes 801897 | solution.py:23
  1116.9 0.8 copy.25
  1117.8 399.9 %while.34 = (s32[]{:T(128)}, f32[256,256]{1,0:T(8,128)S(1)}, f32[256,256]{1,0:T(8,128)S(1)}, s32[]{:T(128)}, s32[]{:T(128)}, /*index=5*/s32[]{:T(128)}) while((s32[]{:T(128)}, f32[256,256]{1,0:T(8,128)S(1)}, f32[256,256]{1,0:T(8,128)S(1)}, s32[]{:T(128)}, s32[]{:T(128)}, /*index=5*/s32[]{:T(128)}) %tuple.85), condition=%wide.region_6.7_spmd.clone.clone, body=%wide.region_5.6_spmd.clone.clone.sunk | while | flops 787971 | bytes 272501 | solution.py:38
  1123.3 0.6 fusion.55
  1129.6 0.6 fusion.55
  1134.2 0.6 fusion.55
  1135.8 0.6 fusion.55
  1140.5 0.6 fusion.55
  1142.1 0.6 fusion.55
  1146.7 0.6 fusion.55
  1153.0 0.6 fusion.55
  1159.2 0.6 fusion.55
  1163.9 0.6 fusion.55
  1165.5 0.6 fusion.55
  1170.2 0.6 fusion.55
  1171.7 0.6 fusion.55
  1176.4 0.6 fusion.55
  1182.7 0.6 fusion.55
  1188.9 0.6 fusion.55
  1193.6 0.6 fusion.55
  1195.2 0.6 fusion.55
  1199.9 0.6 fusion.55
  1201.4 0.6 fusion.55
  1206.1 0.6 fusion.55
  1212.4 0.6 fusion.55
  1218.6 0.6 fusion.55
  1223.3 0.6 fusion.55
  1224.9 0.6 fusion.55
  1229.5 0.6 fusion.55
  1231.1 0.6 fusion.55
  1235.8 0.6 fusion.55
  1242.0 0.6 fusion.55
  1517.7 1.0 fusion.31
  1518.7 0.7 copy.50
  (3837 shorter events, 808.1 us)
Async XLA Ops:
  7.2 55.7 %copy-start = (f32[1,1,2,256,256]{4,3,2,1,0:T(8,128)S(1)}, f32[1,1,2,256,256]{4,3,2,1,0:T(8,128)}, u32[]{:S(2)}) copy-start(f32[1,1,2,256,256]{4,3,2,1,0:T(8,128)} %param.10) | copy-start | bytes 1572868
  7.2 53.8 %all-gather.2.cloned.1.call-start = ((), (), s32[]{:S(2)}) async-start(), calls=%async_computation.1 | async-start | bytes 1081344 | tf_op jit(solution)/shard_map/all_gather | solution.py:45
  7.9 0.7 copy-start.3
  7.9 131.7 %all-reduce.3.cloned.1.call-start = ((), (), s32[]{:S(2)}) async-start(), calls=%async_computation.2 | async-start | bytes 524288 | tf_op jit(solution)/shard_map/psum | solution.py:72
  64.1 0.7 copy-start.4
  67.4 161.2 %reduce-scatter.2.cloned.1.call-start = ((), (), s32[]{:S(2)}) async-start(), calls=%async_computation.3 | async-start | bytes 1081344 | tf_op jit(solution)/shard_map/reduce_scatter | solution.py:92
  145.1 339.4 %all-reduce.5.cloned.1.call-start = ((), (), s32[]{:S(2)}) async-start(), calls=%async_computation.4 | async-start | bytes 524288 | tf_op jit(solution)/shard_map/psum | solution.py:98
  1117.8 399.9 %copy-start.2 = (f32[32,256]{1,0:T(8,128)S(1)}, f32[32,256]{1,0:T(8,128)}, u32[]{:S(2)}) copy-start(f32[32,256]{1,0:T(8,128)} %reduce-scatter.2.cloned.1.call-done) | copy-start | bytes 98308
  1517.7 1.0 copy-start.1
Sparse Core Ops, SparseCore 0:
  10.6 50.4 all-gather.1
  67.5 72.1 all-reduce.2
  145.3 83.2 reduce-scatter.1
  234.4 250.0 all-reduce.4
where the time goes:
time: 1530 us
  local copies, waits for them, and re-layouts  539 us (35%)
  waiting for transfers between devices  463 us (30%)
  loops' own time  206 us (13%)
  other arithmetic  177 us (12%)
  matrix products  126 us (8%)
    psum x1, waiting for transfers between devices, body(): gram_matrix = lax.psum(local_gram, ('row', 'col')) / matrix_order  254 us
    another operation x1, loops' own time, cholesky_lower(): return lax.fori_loop(0, size, column_step, jnp.zeros_like(gram))  195 us
    div x256, other arithmetic, row_step(): (unit - jnp.dot(known, inverse, precision=lax.Precision.HIGHEST)) / pivot  166 us
    dynamic_slice x256, local copies, waits for them, and re-layouts, row_step(): pivot = lax.dynamic_slice_in_dim(row_l, i, 1, 0)[0]  161 us
    dynamic_update_slice x256, local copies, waits for them, and re-layouts, column_step(): return lax.dynamic_update_slice_in_dim(lower, column[:, None], j, 1)  157 us
    dynamic_slice x256, local copies, waits for them, and re-layouts, column_step(): pivot = jnp.sqrt(lax.dynamic_slice_in_dim(column, j, 1, 0)[0])  151 us
    reduce_scatter x1, waiting for transfers between devices, body(): lax.psum_scatter(partial_flat, 'row', scatter_dimension=0, tiled=True)  83.4 us
    psum x1, waiting for transfers between devices, body(): image_block = lax.psum(partial_rows, 'col')  72.3 us
  transfers between devices with their start and end apart: 4, of which 4 were waited for; matrix products, arithmetic and copies ran while one was open for 0% of the time, Pallas kernels for 0%

commit v1 on v0

--- a/solution.py
+++ b/solution.py
@@ -42,7 +42,10 @@
     tile_size = tile_values.shape[-1]
     basis_width = start_block.shape[1]
     slot_total = tile_values.shape[2]
-    slab = lax.all_gather(start_block, "row", axis=0, tiled=True)
+    count = lax.axis_size("row")
+    tiles = jnp.stack([start_block for _ in range(count)])
+    tiles = lax.all_to_all(tiles, "row", split_axis=0, concat_axis=0)
+    slab = jnp.concatenate(tiles, axis=0)
     start_blocks = slab.reshape(-1, tile_size, basis_width)
     block_cols = start_blocks.shape[0]
     values = tile_values.reshape(slot_total, tile_size, tile_size)

time: 1530 us -> 1500 us (0.980)
  waiting for transfers between devices: 463 us -> 426 us
    all_gather x1 -> x0, waiting for transfers between devices: 52.4 us -> none  [body(): slab = lax.all_gather(start_block, 'row', axis=0, tiled=True)]
    all_to_all x0 -> x1, waiting for transfers between devices: none -> 15.4 us  [body(): tiles = lax.all_to_all(tiles, 'row', split_axis=0, concat_axis=0)]
where the time goes in v1:
time: 1500 us
  local copies, waits for them, and re-layouts  540 us (36%)
  waiting for transfers between devices  426 us (28%)
  loops' own time  206 us (14%)
  other arithmetic  177 us (12%)
  matrix products  126 us (8%)
    psum x1, waiting for transfers between devices, body(): gram_matrix = lax.psum(local_gram, ('row', 'col')) / matrix_order  254 us
    another operation x1, loops' own time, cholesky_lower(): return lax.fori_loop(0, size, column_step, jnp.zeros_like(gram))  195 us
    div x256, other arithmetic, row_step(): (unit - jnp.dot(known, inverse, precision=lax.Precision.HIGHEST)) / pivot  166 us
    dynamic_slice x256, local copies, waits for them, and re-layouts, row_step(): pivot = lax.dynamic_slice_in_dim(row_l, i, 1, 0)[0]  161 us
    dynamic_update_slice x256, local copies, waits for them, and re-layouts, column_step(): return lax.dynamic_update_slice_in_dim(lower, column[:, None], j, 1)  157 us
    dynamic_slice x256, local copies, waits for them, and re-layouts, column_step(): pivot = jnp.sqrt(lax.dynamic_slice_in_dim(column, j, 1, 0)[0])  151 us
    reduce_scatter x1, waiting for transfers between devices, body(): lax.psum_scatter(partial_flat, 'row', scatter_dimension=0, tiled=True)  83.4 us
    psum x1, waiting for transfers between devices, body(): image_block = lax.psum(partial_rows, 'col')  72.7 us
  transfers between devices with their start and end apart: 4, of which 4 were waited for; matrix products, arithmetic and copies ran while one was open for 0% of the time, Pallas kernels for 0%

profile of v1, /device:TPU:2, one launch (start us, length us, event | category | flops | bytes accessed | tf_op | source)
XLA Modules:
  0.0 1497.0 jit_solution(10159560361448486694)
XLA Ops:
  7.2 1.9 stack.2
  9.1 7.6 all-to-all-start
  17.4 15.4 %all-to-all-done = f32[32,32,256]{2,1,0:T(8,128)S(1)} async-done(((f32[32,32,256]{2,1,0:T(8,128)}), f32[32,32,256]{2,1,0:T(8,128)S(1)}, u32[]{:S(2)}, u32[]{:S(2)}) %all-to-all-start) | async-done | bytes 1048608 | tf_op jit(solution)/shard_map/all_to_all | solution.py:47
  33.4 1.0 convolution_bitcast_fusion.1
  35.4 1.8 fusion.22
  37.2 0.7 copy.30
  38.0 72.7 %all-reduce.3.cloned.1.call-done = f32[256,256]{1,0:T(8,128)} async-done(((f32[256,256]{1,0:T(8,128)}), f32[256,256]{1,0:T(8,128)}) %all-reduce.3.cloned.1.call-update) | async-done | bytes 262160 | tf_op jit(solution)/shard_map/psum | solution.py:75
  110.7 1.1 copy.21
  112.6 2.3 fusion.14
  114.9 1.2 copy.23
  116.2 83.4 %reduce-scatter.2.cloned.1.call-done = f32[32,256]{1,0:T(8,128)} async-done(((f32[1024,256]{1,0:T(8,128)}), f32[32,256]{1,0:T(8,128)}) %reduce-scatter.2.cloned.1.call-update) | async-done | bytes 32784 | tf_op jit(solution)/shard_map/reduce_scatter | solution.py:95
  199.5 2.0 fusion.30
  201.5 254.1 %all-reduce.5.cloned.1.call-done = f32[256,256]{1,0:T(8,128)} async-done(((f32[256,256]{1,0:T(8,128)}), f32[256,256]{1,0:T(8,128)}) %all-reduce.5.cloned.1.call-update) | async-done | bytes 262160 | tf_op jit(solution)/shard_map/psum | solution.py:101
  455.6 1.0 broadcast_multiply_fusion.1
  456.7 631.3 %while.33 = (s32[]{:T(128)}, f32[256,256]{1,0:T(8,128)S(1)}, f32[256,256]{0,1:T(8,128)S(1)}, s32[]{:T(128)}, s32[]{:T(128)}) while((s32[]{:T(128)}, f32[256,256]{1,0:T(8,128)S(1)}, f32[256,256]{0,1:T(8,128)S(1)}, s32[]{:T(128)}, s32[]{:T(128)}) %tuple.82), condition=%wide.region_4.5_spmd.clone.clone, body=%wide.region_3.4_spmd.clone.clone.sunk | while | flops 853506 | bytes 801897 | solution.py:23
  1088.0 0.8 copy.25
  1088.8 399.9 %while.34 = (s32[]{:T(128)}, f32[256,256]{1,0:T(8,128)S(1)}, f32[256,256]{1,0:T(8,128)S(1)}, s32[]{:T(128)}, s32[]{:T(128)}, /*index=5*/s32[]{:T(128)}) while((s32[]{:T(128)}, f32[256,256]{1,0:T(8,128)S(1)}, f32[256,256]{1,0:T(8,128)S(1)}, s32[]{:T(128)}, s32[]{:T(128)}, /*index=5*/s32[]{:T(128)}) %tuple.85), condition=%wide.region_6.7_spmd.clone.clone, body=%wide.region_5.6_spmd.clone.clone.sunk | while | flops 787971 | bytes 272501 | solution.py:38
  1089.7 0.6 fusion.55
  1094.4 0.6 fusion.55
  1100.6 0.6 fusion.55
  1106.9 0.6 fusion.55
  1111.6 0.6 fusion.55
  1113.1 0.6 fusion.55
  1117.8 0.6 fusion.55
  1119.4 0.6 fusion.55
  1124.1 0.6 fusion.55
  1130.3 0.6 fusion.55
  1136.6 0.6 fusion.55
  1141.2 0.6 fusion.55
  1142.8 0.6 fusion.55
  1147.5 0.6 fusion.55
  1149.0 0.6 fusion.55
  1153.7 0.6 fusion.55
  1160.0 0.6 fusion.55
  1166.2 0.6 fusion.55
  1170.9 0.6 fusion.55
  1172.5 0.6 fusion.55
  1177.2 0.6 fusion.55
  1178.7 0.6 fusion.55
  1183.4 0.6 fusion.55
  1189.7 0.6 fusion.55
  1195.9 0.6 fusion.55
  1200.6 0.6 fusion.55
  1202.2 0.6 fusion.55
  1206.8 0.6 fusion.55
  1208.4 0.6 fusion.55
  1488.8 1.0 fusion.31
  1489.7 0.7 copy.50
  (3837 shorter events, 808.6 us)
Async XLA Ops:
  7.2 26.2 %copy-start = (f32[1,1,2,256,256]{4,3,2,1,0:T(8,128)S(1)}, f32[1,1,2,256,256]{4,3,2,1,0:T(8,128)}, u32[]{:S(2)}) copy-start(f32[1,1,2,256,256]{4,3,2,1,0:T(8,128)} %param.10) | copy-start | bytes 1572868
  9.1 23.7 %all-to-all-start = ((f32[32,32,256]{2,1,0:T(8,128)}), f32[32,32,256]{2,1,0:T(8,128)S(1)}, u32[]{:S(2)}, u32[]{:S(2)}) async-start(f32[32,32,256]{2,1,0:T(8,128)} %stack.2), calls=%async_computation | async-start | bytes 2097152 | tf_op jit(solution)/shard_map/all_to_all | solution.py:47
  16.7 0.7 copy-start.3
  16.7 94.0 %all-reduce.3.cloned.1.call-start = ((), (), s32[]{:S(2)}) async-start(), calls=%async_computation.2 | async-start | bytes 524288 | tf_op jit(solution)/shard_map/psum | solution.py:75
  34.7 0.7 copy-start.4
  37.9 161.6 %reduce-scatter.2.cloned.1.call-start = ((), (), s32[]{:S(2)}) async-start(), calls=%async_computation.3 | async-start | bytes 1081344 | tf_op jit(solution)/shard_map/reduce_scatter | solution.py:95
  116.1 339.4 %all-reduce.5.cloned.1.call-start = ((), (), s32[]{:S(2)}) async-start(), calls=%async_computation.4 | async-start | bytes 524288 | tf_op jit(solution)/shard_map/psum | solution.py:101
  1088.8 399.9 %copy-start.2 = (f32[32,256]{1,0:T(8,128)S(1)}, f32[32,256]{1,0:T(8,128)}, u32[]{:S(2)}) copy-start(f32[32,256]{1,0:T(8,128)} %reduce-scatter.2.cloned.1.call-done) | copy-start | bytes 98308
  1488.7 1.0 copy-start.1
Sparse Core Ops, SparseCore 0:
  38.0 72.5 all-reduce.2
  116.2 83.2 reduce-scatter.1
  205.6 249.9 all-reduce.4

commit v2 on v0

--- a/solution.py
+++ b/solution.py
@@ -4,6 +4,11 @@
 from jax.sharding import PartitionSpec as P
 
 BR = 1
+
+
+def by_each_axis(value, first, second):
+    half = lax.psum(value, first)
+    return lax.psum(half, second)
 
 
 def cholesky_lower(gram):
@@ -95,7 +100,7 @@
     local_gram = jnp.dot(
         projected.T, projected, precision=lax.Precision.HIGHEST, preferred_element_type=jnp.float32
     )
-    gram_matrix = lax.psum(local_gram, ("row", "col")) / matrix_order
+    gram_matrix = by_each_axis(local_gram, "row", "col") / matrix_order
     lower = cholesky_lower(gram_matrix)
     inverse = lower_inverse(lower)
     factor = lower.T

time: 1530 us -> 1460 us (0.954)
  waiting for transfers between devices: 463 us -> 396 us
    psum x1 -> x2, waiting for transfers between devices: 254 us -> 187 us  [the longest x1 112 us: by_each_axis(): half = lax.psum(value, first)]
  transfers between devices with their start and end apart: 4 -> 5, of which waited for: 4 -> 5; matrix products, arithmetic and copies ran while one was open for 0% -> 0% of each run, Pallas kernels for 0% -> 0%
where the time goes in v2:
time: 1460 us
  local copies, waits for them, and re-layouts  539 us (37%)
  waiting for transfers between devices  396 us (27%)
  loops' own time  206 us (14%)
  other arithmetic  177 us (12%)
  matrix products  126 us (9%)
  between operations  14.6 us (1%)
    another operation x1, loops' own time, cholesky_lower(): return lax.fori_loop(0, size, column_step, jnp.zeros_like(gram))  195 us
    div x256, other arithmetic, row_step(): (unit - jnp.dot(known, inverse, precision=lax.Precision.HIGHEST)) / pivot  166 us
    dynamic_slice x256, local copies, waits for them, and re-layouts, row_step(): pivot = lax.dynamic_slice_in_dim(row_l, i, 1, 0)[0]  161 us
    dynamic_update_slice x256, local copies, waits for them, and re-layouts, column_step(): return lax.dynamic_update_slice_in_dim(lower, column[:, None], j, 1)  157 us
    dynamic_slice x256, local copies, waits for them, and re-layouts, column_step(): pivot = jnp.sqrt(lax.dynamic_slice_in_dim(column, j, 1, 0)[0])  151 us
    psum x1, waiting for transfers between devices, by_each_axis(): half = lax.psum(value, first)  112 us
    reduce_scatter x1, waiting for transfers between devices, body(): lax.psum_scatter(partial_flat, 'row', scatter_dimension=0, tiled=True)  83.3 us
    psum x1, waiting for transfers between devices, by_each_axis(): return lax.psum(half, second)  75 us
  transfers between devices with their start and end apart: 5, of which 5 were waited for; matrix products, arithmetic and copies ran while one was open for 0% of the time, Pallas kernels for 0%

profile of v2, /device:TPU:2, one launch (start us, length us, event | category | flops | bytes accessed | tf_op | source)
XLA Modules:
  0.0 1459.3 jit_solution(12827107235651050421)
XLA Ops:
  7.2 0.7 all-gather.2.cloned.1.call-update
  8.7 52.4 %all-gather.2.cloned.1.call-done = f32[1024,256]{1,0:T(8,128)} async-done(((f32[32,256]{1,0:T(8,128)}), f32[1024,256]{1,0:T(8,128)}) %all-gather.2.cloned.1.call-update) | async-done | bytes 1048592 | tf_op jit(solution)/shard_map/all_gather | solution.py:50
  61.0 1.8 gather_fusion
  62.8 1.0 convolution_bitcast_fusion.1
  64.8 1.8 fusion.22
  66.6 0.7 copy.30
  67.4 72.3 %all-reduce.4.cloned.1.call-done = f32[256,256]{1,0:T(8,128)} async-done(((f32[256,256]{1,0:T(8,128)}), f32[256,256]{1,0:T(8,128)}) %all-reduce.4.cloned.1.call-update) | async-done | bytes 262160 | tf_op jit(solution)/shard_map/psum | solution.py:77
  139.7 1.1 copy.21
  141.6 2.3 fusion.14
  143.9 1.2 copy.23
  145.2 83.3 %reduce-scatter.2.cloned.1.call-done = f32[32,256]{1,0:T(8,128)} async-done(((f32[1024,256]{1,0:T(8,128)}), f32[32,256]{1,0:T(8,128)}) %reduce-scatter.2.cloned.1.call-update) | async-done | bytes 32784 | tf_op jit(solution)/shard_map/reduce_scatter | solution.py:97
  228.5 1.9 fusion.30
  230.5 112.3 %all-reduce.6.cloned.1.call-done = f32[256,256]{1,0:T(8,128)} async-done(((f32[256,256]{1,0:T(8,128)}), f32[256,256]{1,0:T(8,128)}) %all-reduce.6.cloned.1.call-update) | async-done | bytes 262160 | tf_op jit(solution)/shard_map/psum | solution.py:10
  342.9 75.0 %all-reduce.8.cloned.1.call-done = f32[256,256]{1,0:T(8,128)} async-done(((f32[256,256]{1,0:T(8,128)}), f32[256,256]{1,0:T(8,128)}) %all-reduce.8.cloned.1.call-update) | async-done | bytes 262160 | tf_op jit(solution)/shard_map/psum | solution.py:11
  417.9 1.0 broadcast_multiply_fusion.1
  419.0 631.3 %while.33 = (s32[]{:T(128)}, f32[256,256]{1,0:T(8,128)S(1)}, f32[256,256]{0,1:T(8,128)S(1)}, s32[]{:T(128)}, s32[]{:T(128)}) while((s32[]{:T(128)}, f32[256,256]{1,0:T(8,128)S(1)}, f32[256,256]{0,1:T(8,128)S(1)}, s32[]{:T(128)}, s32[]{:T(128)}) %tuple.82), condition=%wide.region_5.6_spmd.clone.clone, body=%wide.region_4.5_spmd.clone.clone.sunk | while | flops 853506 | bytes 801897 | solution.py:28
  1050.3 0.8 copy.25
  1051.2 399.9 %while.34 = (s32[]{:T(128)}, f32[256,256]{1,0:T(8,128)S(1)}, f32[256,256]{1,0:T(8,128)S(1)}, s32[]{:T(128)}, s32[]{:T(128)}, /*index=5*/s32[]{:T(128)}) while((s32[]{:T(128)}, f32[256,256]{1,0:T(8,128)S(1)}, f32[256,256]{1,0:T(8,128)S(1)}, s32[]{:T(128)}, s32[]{:T(128)}, /*index=5*/s32[]{:T(128)}) %tuple.85), condition=%wide.region_7.8_spmd.clone.clone, body=%wide.region_6.7_spmd.clone.clone.sunk | while | flops 787971 | bytes 272501 | solution.py:43
  1055.1 0.6 fusion.55
  1059.8 0.6 fusion.55
  1061.4 0.6 fusion.55
  1066.1 0.6 fusion.55
  1067.6 0.6 fusion.55
  1072.3 0.6 fusion.55
  1078.6 0.6 fusion.55
  1084.8 0.6 fusion.55
  1089.5 0.6 fusion.55
  1091.1 0.6 fusion.55
  1095.7 0.6 fusion.55
  1097.3 0.6 fusion.55
  1102.0 0.6 fusion.55
  1108.2 0.6 fusion.55
  1114.5 0.6 fusion.55
  1119.2 0.6 fusion.55
  1120.7 0.6 fusion.55
  1125.4 0.6 fusion.55
  1127.0 0.6 fusion.55
  1131.7 0.6 fusion.55
  1137.9 0.6 fusion.55
  1144.2 0.6 fusion.55
  1148.9 0.6 fusion.55
  1150.4 0.6 fusion.55
  1155.1 0.6 fusion.55
  1156.7 0.6 fusion.55
  1161.4 0.6 fusion.55
  1167.6 0.6 fusion.55
  1451.1 1.0 fusion.31
  1452.0 0.7 copy.51
  (3840 shorter events, 808.8 us)
Async XLA Ops:
  7.2 55.7 %copy-start = (f32[1,1,2,256,256]{4,3,2,1,0:T(8,128)S(1)}, f32[1,1,2,256,256]{4,3,2,1,0:T(8,128)}, u32[]{:S(2)}) copy-start(f32[1,1,2,256,256]{4,3,2,1,0:T(8,128)} %param.10) | copy-start | bytes 1572868
  7.2 53.8 %all-gather.2.cloned.1.call-start = ((), (), s32[]{:S(2)}) async-start(), calls=%async_computation.1 | async-start | bytes 1081344 | tf_op jit(solution)/shard_map/all_gather | solution.py:50
  7.9 0.7 copy-start.3
  7.9 131.7 %all-reduce.4.cloned.1.call-start = ((), (), s32[]{:S(2)}) async-start(), calls=%async_computation.2 | async-start | bytes 524288 | tf_op jit(solution)/shard_map/psum | solution.py:77
  64.1 0.7 copy-start.4
  67.4 161.2 %reduce-scatter.2.cloned.1.call-start = ((), (), s32[]{:S(2)}) async-start(), calls=%async_computation.3 | async-start | bytes 1081344 | tf_op jit(solution)/shard_map/reduce_scatter | solution.py:97
  145.1 197.7 %all-reduce.6.cloned.1.call-start = ((), (), s32[]{:S(2)}) async-start(), calls=%async_computation.4 | async-start | bytes 524288 | tf_op jit(solution)/shard_map/psum | solution.py:10
  230.5 187.4 %all-reduce.8.cloned.1.call-start = ((), (), s32[]{:S(2)}) async-start(), calls=%async_computation.5 | async-start | bytes 524288 | tf_op jit(solution)/shard_map/psum | solution.py:11
  1051.1 399.9 %copy-start.2 = (f32[32,256]{1,0:T(8,128)S(1)}, f32[32,256]{1,0:T(8,128)}, u32[]{:S(2)}) copy-start(f32[32,256]{1,0:T(8,128)} %reduce-scatter.2.cloned.1.call-done) | copy-start | bytes 98308
  1451.1 1.0 copy-start.1
Sparse Core Ops, SparseCore 0:
  10.6 50.4 all-gather.1
  67.5 72.1 all-reduce.3
  145.3 83.2 reduce-scatter.1
  232.2 110.6 all-reduce.5
  345.1 72.7 all-reduce.7
